TPU v7x, 32 devices: a whole 2x2x4 slice. The times are simulated.
32 devices in a mesh: expert: 8 (over z, x), tensor: 4 (over y, core).
Axes of the slice: x: 2, y: 2, z: 4, core: 2. Of those that a mesh axis runs over, the one named last changes fastest.
Arguments:
- context: bfloat16 [2048, 2048], P('expert', 'tensor'), may hold values from -0.25976562 to 0.25976562
- out_proj: bfloat16 [2048, 2048], P('tensor'), may hold values from -0.125 to 0.125
- residual: bfloat16 [2048, 2048], P(('expert', 'tensor')), may hold values from -0.25976562 to 0.25976562
- norm_gain: float32 [2048], replicated, may hold values from 0.1 to 1.9
- router_weight: float32 [2048, 64], replicated, may hold values from -5.524272 to 5.524272
- expert_ids: int32 [2048, 8], P('expert'), may hold values from 0 to 63, all different within a row; in each aligned block of 64 rows (0 to 63, 64 to 127, ...) at most 10 rows name the same one
- placement: int32 [128], replicated, may hold values from 0 to 63, as said below
- expert_weights: bfloat16 [128, 3, 2048, 1024], P('expert', None, None, 'tensor'), as said below
- post_gain: float32 [2048], replicated, may hold values from 0.5 to 1.5
Outputs:
- hidden_out: float32 [2048, 2048], P(('expert', 'tensor'))
- normed_out: float32 [2048, 2048], P(('expert', 'tensor'))
Inputs may be any that keep to these rules, and one draw needn't show every extreme that they name: `expert_ids`: each row names 8 different experts. In each aligned block of 64 rows (the rows of one device) no expert is named by more than 10 rows, a bound that some block reaches; every expert is named somewhere. `placement`: every expert is held by one, three or five slots. `expert_weights`: slots that hold the same expert carry equal weights.
All inputs are finite; a program needn't handle non-finite values.
Results may differ from a plain program's by a relative error of at most 0.018.
Values may be sent and summed in bfloat16 or wider, within the bound.
No kernel may reach another device: no remote copies, remote signals or barrier semaphores. Data moves between devices by JAX's collectives and lax.ppermute only.
A program may use at most 256 MiB of HBM per device.

v0:
```python
import jax
import jax.numpy as jnp
from jax import lax
from jax.sharding import PartitionSpec as P

EPS = 1e-06


def rms_scale(values, gain_row):
    mean_square = jnp.mean(values * values, axis=-1, keepdims=True)
    return values * lax.rsqrt(mean_square + EPS) * gain_row


def expert_partial(block_rows, weights):
    gate_pre = jnp.einsum(
        "nqsmd,sdf->nqsmf", block_rows, weights[:, 0], preferred_element_type=jnp.float32
    )
    up_pre = jnp.einsum(
        "nqsmd,sdf->nqsmf", block_rows, weights[:, 1], preferred_element_type=jnp.float32
    )
    inner_act = (jax.nn.silu(gate_pre) * up_pre).astype(jnp.bfloat16)
    return jnp.einsum(
        "nqsmf,sdf->nqsmd", inner_act, weights[:, 2], preferred_element_type=jnp.float32
    )


def on_device(
    context,
    out_proj,
    residual,
    norm_gain,
    router_weight,
    expert_ids,
    placement,
    expert_weights,
    post_gain,
):
    groups = lax.axis_size("tensor")
    holders = lax.axis_size("expert")
    my_group = lax.axis_index("tensor")
    my_holder = lax.axis_index("expert")
    row_count = residual.shape[0]
    model_width = residual.shape[1]
    top_count = expert_ids.shape[1]
    expert_count = router_weight.shape[1]
    slot_dev = expert_weights.shape[0]
    slot_total = placement.shape[0]
    blocks = holders * groups
    capacity = max(2, row_count * top_count * 5 // (expert_count * 4))
    expert_range = jnp.arange(expert_count, dtype=jnp.int32)
    slot_range = jnp.arange(slot_total, dtype=jnp.int32)
    attention = lax.psum_scatter(
        jnp.dot(context, out_proj, preferred_element_type=jnp.float32).astype(jnp.bfloat16),
        "tensor",
        scatter_dimension=0,
        tiled=True,
    ).astype(jnp.float32)
    hidden_mid = residual.astype(jnp.float32) + attention
    normed_full = rms_scale(hidden_mid, norm_gain)
    normed = normed_full.astype(jnp.bfloat16)
    logits = jnp.dot(normed_full, router_weight, precision=lax.Precision.HIGHEST)
    own_ids = lax.dynamic_slice_in_dim(expert_ids, my_group * row_count, row_count, 0)
    own_onehot = own_ids[:, :, None] == expert_range[None, None, :]
    chosen = jnp.sum(jnp.where(own_onehot, logits[:, None, :], 0.0), axis=-1)
    gate_weights = jax.nn.softmax(chosen, axis=-1)
    all_rows = lax.all_gather(normed, ("expert", "tensor"), axis=0, tiled=True)
    all_ids = lax.all_gather(expert_ids, "expert", axis=0, tiled=True)
    holds = (placement[None, :] == expert_range[:, None]).astype(jnp.int32)
    copies = jnp.sum(holds, axis=1)
    copy_rank = jnp.cumsum(holds, axis=1) - 1
    holder_range = jnp.arange(holders, dtype=jnp.int32)
    copy_pick = holder_range[:, None] % copies[None, :]
    picked = (holds[None] > 0) & (copy_rank[None] == copy_pick[:, :, None])
    slot_pick = jnp.sum(jnp.where(picked, slot_range[None, None, :], 0), axis=2)
    flat_ids = all_ids.reshape(blocks, row_count * top_count)
    block_holder = jnp.arange(blocks, dtype=jnp.int32) // groups
    block_pick = slot_pick[block_holder]
    onehot = flat_ids[:, :, None] == expert_range
    slot_of = jnp.sum(jnp.where(onehot, block_pick[:, None, :], 0), axis=-1)
    slot_hot = (slot_of[:, :, None] == slot_range).astype(jnp.int32)
    rank_all = jnp.sum(jnp.cumsum(slot_hot, axis=1) * slot_hot, axis=-1) - 1
    holder_all = slot_of // slot_dev
    local_all = slot_of % slot_dev
    block_ids = jnp.arange(blocks, dtype=jnp.int32)[:, None]
    token_of = (
        block_ids * row_count
        + jnp.arange(row_count * top_count, dtype=jnp.int32)[None, :] // top_count
    )
    mine = holder_all == my_holder
    row_total = blocks * slot_dev * capacity
    target = jnp.where(mine, (block_ids * slot_dev + local_all) * capacity + rank_all, row_total)
    index_table = (
        jnp.zeros((row_total,), jnp.int32)
        .at[target.reshape(-1)]
        .set(token_of.reshape(-1), mode="drop", unique_indices=True)
    )
    received = jnp.take(all_rows, index_table, axis=0).reshape(
        holders, groups, slot_dev, capacity, model_width
    )
    own_block = my_holder * groups + my_group
    holder = lax.dynamic_index_in_dim(holder_all, own_block, 0, keepdims=False)
    local_slot = lax.dynamic_index_in_dim(local_all, own_block, 0, keepdims=False)
    rank_in = lax.dynamic_index_in_dim(rank_all, own_block, 0, keepdims=False)
    partial_value = expert_partial(received, expert_weights)
    expert_sum = lax.psum_scatter(
        partial_value.astype(jnp.bfloat16), "tensor", scatter_dimension=1, tiled=True
    )
    returned = lax.all_to_all(expert_sum, "expert", split_axis=0, concat_axis=0, tiled=True)
    own_index = (holder * slot_dev + local_slot) * capacity + rank_in
    outputs = returned.reshape(-1, model_width)[own_index].reshape(
        row_count, top_count, model_width
    )
    moe_sum = jnp.einsum("rk,rkd->rd", gate_weights, outputs.astype(jnp.float32))
    hidden_out = hidden_mid + moe_sum
    normed_out = rms_scale(hidden_out, post_gain)
    return (hidden_out, normed_out)


def solution(mesh):
    in_specs = (
        P("expert", "tensor"),
        P("tensor", None),
        P(("expert", "tensor"), None),
        P(),
        P(),
        P("expert", None),
        P(),
        P("expert", None, None, "tensor"),
        P(),
    )
    out_specs = (P(("expert", "tensor"), None), P(("expert", "tensor"), None))
    return jax.shard_map(
        on_device, mesh=mesh, in_specs=in_specs, out_specs=out_specs, check_vma=False
    )
```

profile of v0, /device:TPU:0, one launch (start us, length us, event | category | flops | bytes accessed | tf_op | source)
XLA Modules:
  0.0 628.9 jit_solution(16265701694805310592)
XLA Ops:
  7.2 0.0 copy-start
  7.2 0.0 copy-start.13
  7.2 0.0 reduce-scatter.3.cloned.1.call-start
  7.2 1.5 copy-done
  8.8 2.7 convolution_convert_fusion
  11.4 0.0 reduce-scatter.3.cloned.1.call-update
  11.4 0.0 all-gather.2.cloned.1.call-start
  11.5 27.7 %reduce-scatter.3.cloned.1.call-done = bf16[64,2048]{1,0:T(8,128)(2,1)} async-done(((bf16[256,2048]{1,0:T(8,128)(2,1)}), bf16[64,2048]{1,0:T(8,128)(2,1)}) %reduce-scatter.3.cloned.1.call-update) | async-done | bytes 262160 | tf_op jit(solution)/shard_map/reduce_scatter | solution.py:52
  39.2 1.2 multiply_reduce_fusion.1
  40.4 1.8 fusion.29
  42.3 0.0 all-gather.2.cloned.1.call-update
  42.3 0.0 reduce-scatter.5.cloned.1.call-start
  42.4 0.1 add_bitcast_fusion
  42.5 0.1 broadcast_bitcast_fusion
  42.6 0.1 copy.88
  42.6 30.9 %all_gather.6 = s32[2048,8]{0,1:T(8,128)S(1)} all-gather(s32[256,8]{0,1:T(8,128)} %param.14), channel_id=1, replica_groups=mesh['expert'=8,'tensor'=4] {'expert'}, dimensions={0}, use_global_device_ids=true | all-gather | bytes 73728 | tf_op jit(solution)/shard_map/all_gather | solution.py:67
  73.5 0.3 copy.65
  73.8 0.5 eq.116
  74.4 0.3 reduce_window_sum.26
  74.7 0.1 fusion.36
  74.8 0.1 add_select_fusion
  75.0 0.3 select_reduce_fusion.2
  75.3 0.6 gather_fusion
  75.9 0.8 select_reduce_fusion.1
  76.7 0.1 copy.66
  76.8 0.1 copy.87
  76.9 2.5 fusion.14
  79.4 1.1 broadcast_add_fusion
  80.5 0.0 copy-done.5
  80.5 11.7 %select_reduce_fusion = s32[32,512]{0,1:T(8,128)S(1)} fusion(s32[32,512,128]{2,0,1:T(8,128)S(1)} %bitcast.112, s32[32,512]{0,1:T(8,128)S(1)} %copy.66), kind=kLoop, calls=%fused_computation.23 | loop fusion | flops 6275072 | bytes 8519680 | tf_op jit(solution)/shard_map/reduce_sum | solution.py:81
  92.2 0.1 copy.68
  92.3 0.7 broadcast_add_fusion.1
  93.0 0.1 copy.89
  93.0 0.6 compare_select_fusion
  93.6 60.5 %scatter_custom_fusion = s32[5120]{0:T(1024)S(1)} fusion(s32[16384]{0:T(1024)S(1)} %bitcast.120, s32[16384]{0:T(1024)S(1)} %bitcast.119, s32[]{:T(128)} %constant.121.clone.1), kind=kCustom, calls=%fused_computation.75 | custom fusion | bytes 20484 | tf_op jit(solution)/shard_map/scatter | solution.py:95
  154.2 0.3 broadcast_in_dim.96
  154.5 0.0 all-gather.2.cloned.1.call-done
  154.5 43.3 %gather_fusion.1 = bf16[5120,2048]{1,0:T(8,128)(2,1)} fusion(bf16[2048,2048]{1,0:T(8,128)(2,1)} %all-gather.2.cloned.1.call-done, s32[5120]{0:T(1024)S(1)} %fusion.38), kind=kCustom, calls=%fused_computation.1 | custom fusion | bytes 41963520 | tf_op jit(solution)/shard_map/jit(_take)/gather | solution.py:97
  197.8 34.0 %gather.14 = bf16[8,4,16,10,2048]{4,3,2,1,0:T(8,128)(2,1)} reshape(bf16[5120,2048]{1,0:T(8,128)(2,1)} %gather_fusion.1) | data formatting | bytes 41943040 | tf_op jit(solution)/shard_map/jit(_take)/gather | solution.py:97
  231.8 20.7 %fusion = f32[16,8,4,10,256]{4,3,2,1,0:T(8,128)} fusion(bf16[16,3,2048,256]{3,2,1,0:T(8,128)(2,1)} %param.16, bf16[8,4,16,10,2048]{4,3,2,1,0:T(8,128)(2,1)} %gather.14, pred[8,4,16,10]{3,2,1,0:T(8,128)(4,1)S(1)} %broadcast_in_dim.96), kind=kOutput, calls=%fused_computation.6 | convolution fusion | flops 5379194880 | bytes 55579648 | tf_op jit(solution)/shard_map/nqsmd,sdf->nqsmf/dot_general | solution.py:18
  252.5 39.2 %convert_bitcast_fusion = bf16[8,4,16,10,2048]{4,3,1,0,2:T(8,128)(2,1)} fusion(bf16[16,3,2048,256]{3,2,1,0:T(8,128)(2,1)} %param.16, f32[16,8,4,10,256]{4,3,2,1,0:T(8,128)} %fusion, bf16[8,4,16,10,2048]{4,3,2,1,0:T(8,128)(2,1)} %gather.14, pred[8,4,16,10]{3,2,1,0:T(8,128)(4,1)S(1)} %broadcast_in_dim.96), kind=kOutput, calls=%fused_computation.4 | convolution fusion | flops 10766254080 | bytes 96474112 | tf_op jit(solution)/shard_map/nqsmf,sdf->nqsmd/dot_general | solution.py:22
  291.7 24.3 %copy.74 = bf16[8,4,16,10,2048]{4,2,3,0,1:T(8,128)(2,1)} copy(bf16[8,4,16,10,2048]{4,3,1,0,2:T(8,128)(2,1)} %convert_bitcast_fusion) | data formatting | bytes 41943040 | tf_op jit(solution)/shard_map/convert_element_type | solution.py:106
  316.0 0.0 reduce-scatter.5.cloned.1.call-update
  316.0 0.0 copy-start.9
  316.1 0.0 copy-start.2
  316.1 0.0 copy-start.7
  316.1 0.0 copy-start.8
  316.1 153.2 %reduce-scatter.5.cloned.1.call-done = bf16[8,1,16,10,2048]{4,2,3,0,1:T(8,128)(2,1)} async-done(((bf16[8,4,16,10,2048]{4,2,3,0,1:T(8,128)(2,1)}), bf16[8,1,16,10,2048]{4,2,3,0,1:T(8,128)(2,1)}) %reduce-scatter.5.cloned.1.call-update) | async-done | bytes 5242896 | tf_op jit(solution)/shard_map/reduce_scatter | solution.py:105
  469.3 5.5 all-to-all-start
  474.9 0.1 constant_dynamic-slice_fusion
  474.9 0.1 copy.62
  475.1 0.8 compare_select_fusion.6
  475.9 0.7 fusion.30
  476.5 0.2 select_reduce_fusion.3
  476.8 0.1 copy.64
  476.8 0.1 reduce_max.9
  477.0 0.1 copy.80
  477.1 113.5 %all-to-all-done = bf16[8,1,16,10,2048]{4,2,3,1,0:T(8,128)(2,1)} async-done(((bf16[8,1,16,10,2048]{4,2,3,1,0:T(8,128)(2,1)}), bf16[8,1,16,10,2048]{4,2,3,1,0:T(8,128)(2,1)}, u32[]{:S(2)}, u32[]{:S(2)}) %all-to-all-start) | async-done | bytes 5242912 | tf_op jit(solution)/shard_map/all_to_all | solution.py:108
  590.6 9.7 %copy.76 = bf16[8,1,16,10,2048]{4,3,2,0,1:T(8,128)(2,1)} copy(bf16[8,1,16,10,2048]{4,2,3,1,0:T(8,128)(2,1)} %all-to-all-done) | data formatting | bytes 10485760 | tf_op jit(solution)/shard_map/all_to_all | solution.py:108
  600.3 10.0 %reshape.449 = bf16[1280,2048]{1,0:T(8,128)(2,1)} reshape(bf16[8,1,16,10,2048]{4,3,2,0,1:T(8,128)(2,1)} %copy.76) | data formatting | bytes 10485760 | tf_op jit(solution)/shard_map/reshape | solution.py:110
  610.3 8.5 %gather_fusion.2 = bf16[512,2048]{1,0:T(8,128)(2,1)} fusion(bf16[1280,2048]{1,0:T(8,128)(2,1)} %reshape.449, s32[1024]{0:T(1024)S(1)} %pad_clamp_fusion), kind=kCustom, calls=%fused_computation.2 | custom fusion | bytes 4196352 | tf_op jit(solution)/shard_map/gather | solution.py:110
  618.8 2.3 fusion.27
  621.1 0.3 multiply_reduce_fusion
  621.4 0.9 multiply_multiply_fusion
  (40 shorter events, 0.2 us)
Async XLA Ops:
  7.2 1.6 copy-start
  7.2 67.2 %copy-start.13 = (s32[128]{0:T(128)S(1)}, s32[128]{0:T(128)}, u32[]{:S(2)}) copy-start(s32[128]{0:T(128)} %param.15) | copy-start | bytes 1540
  7.2 32.0 %reduce-scatter.3.cloned.1.call-start = ((), (), s32[]{:S(2)}) async-start(), calls=%async_computation.3 | async-start | bytes 1310720 | tf_op jit(solution)/shard_map/reduce_scatter | solution.py:52
  11.4 143.0 %all-gather.2.cloned.1.call-start = ((), (), s32[]{:S(2)}) async-start(), calls=%async_computation.4 | async-start | bytes 8650752 | tf_op jit(solution)/shard_map/all_gather | solution.py:66
  40.4 2.0 copy-start.11
  42.3 427.0 %reduce-scatter.5.cloned.1.call-start = ((), (), s32[]{:S(2)}) async-start(), calls=%async_computation.5 | async-start | bytes 26214400 | tf_op jit(solution)/shard_map/reduce_scatter | solution.py:105
  76.7 3.8 copy-start.5
  316.0 158.8 %copy-start.9 = (s32[256,8]{0,1:T(8,128)S(1)}, s32[256,8]{0,1:T(8,128)}, u32[]{:S(2)}) copy-start(s32[256,8]{0,1:T(8,128)} %param.14) | copy-start | bytes 24580
  316.0 159.0 %copy-start.6 = (s32[32,512]{1,0:T(8,128)S(1)}, s32[32,512]{1,0:T(8,128)}, u32[]{:S(2)}) copy-start(s32[32,512]{1,0:T(8,128)} %copy-done.5) | copy-start | bytes 196612
  316.1 159.8 %copy-start.2 = (bf16[64,2048]{1,0:T(8,128)(2,1)S(1)}, bf16[64,2048]{1,0:T(8,128)(2,1)}, u32[]{:S(2)}) copy-start(bf16[64,2048]{1,0:T(8,128)(2,1)} %param.11) | copy-start | bytes 786436
  316.1 159.8 %copy-start.3 = (bf16[64,2048]{1,0:T(8,128)(2,1)S(1)}, bf16[64,2048]{1,0:T(8,128)(2,1)}, u32[]{:S(2)}) copy-start(bf16[64,2048]{1,0:T(8,128)(2,1)} %reduce-scatter.3.cloned.1.call-done) | copy-start | bytes 786436
  316.1 159.8 %copy-start.7 = (f32[2048,64]{0,1:T(8,128)S(1)}, f32[2048,64]{0,1:T(8,128)}, u32[]{:S(2)}) copy-start(f32[2048,64]{0,1:T(8,128)} %param.13) | copy-start | bytes 1572868
  316.1 159.8 %copy-start.8 = (f32[2048]{0:T(1024)S(1)}, f32[2048]{0:T(1024)}, u32[]{:S(2)}) copy-start(f32[2048]{0:T(1024)} %param.12) | copy-start | bytes 24580
  316.1 159.8 %copy-start.12 = (f32[64]{0:T(128)S(1)}, f32[64]{0:T(128)}, u32[]{:S(2)}) copy-start(f32[64]{0:T(128)} %copy-done.11) | copy-start | bytes 772
  469.3 121.3 %all-to-all-start = ((bf16[8,1,16,10,2048]{4,2,3,1,0:T(8,128)(2,1)}), bf16[8,1,16,10,2048]{4,2,3,1,0:T(8,128)(2,1)}, u32[]{:S(2)}, u32[]{:S(2)}) async-start(bf16[8,1,16,10,2048]{4,2,3,1,0:T(8,128)(2,1)} %bitcast.113), calls=%async_computation.2 | async-start | bytes 10485760 | tf_op jit(solution)/shard_map/all_to_all | solution.py:108
  600.3 22.0 %copy-start.1 = (bf16[512,2048]{1,0:T(8,128)(2,1)S(1)}, bf16[512,2048]{1,0:T(8,128)(2,1)}, u32[]{:S(2)}) copy-start(bf16[512,2048]{1,0:T(8,128)(2,1)} %param.10) | copy-start | bytes 6291460
  610.3 11.1 %copy-start.10 = (f32[2048]{0:T(1024)S(1)}, f32[2048]{0:T(1024)}, u32[]{:S(2)}) copy-start(f32[2048]{0:T(1024)} %param.17) | copy-start | bytes 24580
  621.4 1.0 copy-start.4
Sparse Core Ops, SparseCore 0:
  11.6 27.5 reduce-scatter.2
  43.0 77.6 all-gather.1
  316.2 153.1 reduce-scatter.4
where the time goes:
time: 631 us; the launch traced here: 629 us
  waiting for transfers between devices  294 us (47%)
  local copies, waits for them, and re-layouts  194 us (31%)
  matrix products  65.5 us (10%)
  blocking collectives  30.9 us (5%)
  other arithmetic  23.8 us (4%)
  between operations  14.2 us (2%)
    reduce_scatter x1, waiting for transfers between devices, on_device(): lax.psum_scatter(partial_value.astype(jnp.bfloat16), 'tensor', scatter_di...  153 us
    all_to_all x1, waiting for transfers between devices, on_device(): lax.all_to_all(expert_sum, 'expert', split_axis=0, concat_axis=0, tiled=T...  113 us
    gather x2, local copies, waits for them, and re-layouts, on_device(): jnp.take(all_rows, index_table, axis=0)  77.3 us
    scatter x1, local copies, waits for them, and re-layouts, on_device(): index_table = jnp.zeros((row_total,), jnp.int32).at[target.reshape(-1)].s...  60.5 us
    dot_general x1, matrix products, expert_partial(): jnp.einsum('nqsmf,sdf->nqsmd', inner_act, weights[:, 2], preferred_elemen...  39.2 us
    all_gather x1, blocking collectives, on_device(): all_ids = lax.all_gather(expert_ids, 'expert', axis=0, tiled=True)  30.9 us
    reduce_scatter x1, waiting for transfers between devices, on_device(): lax.psum_scatter(jnp.dot(context, out_proj, preferred_element_type=jnp.fl...  27.7 us
    convert_element_type x1, local copies, waits for them, and re-layouts, on_device(): partial_value.astype(jnp.bfloat16)  24.3 us
  transfers between devices with their start and end apart: 4, of which 3 were waited for; matrix products, arithmetic and copies ran while one was open for 13% of the time, Pallas kernels for 0%

commit v1 on v0

--- a/solution.py
+++ b/solution.py
@@ -64,7 +64,13 @@
     chosen = jnp.sum(jnp.where(own_onehot, logits[:, None, :], 0.0), axis=-1)
     gate_weights = jax.nn.softmax(chosen, axis=-1)
     all_rows = lax.all_gather(normed, ("expert", "tensor"), axis=0, tiled=True)
-    all_ids = lax.all_gather(expert_ids, "expert", axis=0, tiled=True)
+    devices = lax.axis_size("expert")
+    held, pieces = (expert_ids, [expert_ids])
+    for _ in range(devices - 1):
+        held = lax.ppermute(held, "expert", [(i, (i + 1) % devices) for i in range(devices)])
+        pieces.insert(0, held)
+    line = jnp.concatenate(pieces, axis=0)
+    all_ids = jnp.roll(line, (lax.axis_index("expert") + 1) * expert_ids.shape[0], axis=0)
     holds = (placement[None, :] == expert_range[:, None]).astype(jnp.int32)
     copies = jnp.sum(holds, axis=1)
     copy_rank = jnp.cumsum(holds, axis=1) - 1

time: 631 us -> 641 us (1.016)
  waiting for transfers between devices: 294 us -> 331 us
  blocking collectives: 30.9 us -> 0 us
    ppermute x0 -> x7, waiting for transfers between devices: none -> 40.4 us  [on_device(): lax.ppermute(held, 'expert', [(i, (i + 1) % devices) for i in range(devic...]
    all_gather x1 -> x0, blocking collectives: 30.9 us -> none  [on_device(): all_ids = lax.all_gather(expert_ids, 'expert', axis=0, tiled=True)]
  transfers between devices with their start and end apart: 4 -> 11, of which waited for: 3 -> 10; matrix products, arithmetic and copies ran while one was open for 13% -> 13% of each run, Pallas kernels for 0% -> 0%
where the time goes in v1:
time: 641 us; the launch traced here: 639 us
  waiting for transfers between devices  331 us (52%)
  local copies, waits for them, and re-layouts  196 us (31%)
  matrix products  65.5 us (10%)
  other arithmetic  25.1 us (4%)
  between operations  14.2 us (2%)
  starting transfers between devices  7.18 us (1%)
    reduce_scatter x1, waiting for transfers between devices, on_device(): lax.psum_scatter(partial_value.astype(jnp.bfloat16), 'tensor', scatter_di...  150 us
    all_to_all x1, waiting for transfers between devices, on_device(): lax.all_to_all(expert_sum, 'expert', split_axis=0, concat_axis=0, tiled=T...  113 us
    gather x2, local copies, waits for them, and re-layouts, on_device(): jnp.take(all_rows, index_table, axis=0)  77.3 us
    scatter x1, local copies, waits for them, and re-layouts, on_device(): index_table = jnp.zeros((row_total,), jnp.int32).at[target.reshape(-1)].s...  60.5 us
    ppermute x7, waiting for transfers between devices, on_device(): lax.ppermute(held, 'expert', [(i, (i + 1) % devices) for i in range(devic...  40.4 us
    dot_general x1, matrix products, expert_partial(): jnp.einsum('nqsmf,sdf->nqsmd', inner_act, weights[:, 2], preferred_elemen...  39.2 us
    reduce_scatter x1, waiting for transfers between devices, on_device(): lax.psum_scatter(jnp.dot(context, out_proj, preferred_element_type=jnp.fl...  27.7 us
    convert_element_type x1, local copies, waits for them, and re-layouts, on_device(): partial_value.astype(jnp.bfloat16)  24.3 us
  transfers between devices with their start and end apart: 11, of which 10 were waited for; matrix products, arithmetic and copies ran while one was open for 13% of the time, Pallas kernels for 0%

profile of v1, /device:TPU:0, one launch (start us, length us, event | category | flops | bytes accessed | tf_op | source)
XLA Modules:
  0.0 639.0 jit_solution(3062658876069556056)
XLA Ops:
  7.2 0.0 reduce-scatter.3.cloned.1.call-start
  7.2 1.5 copy-done
  8.8 2.7 convolution_convert_fusion
  11.4 0.0 all-gather.2.cloned.1.call-start
  11.5 27.7 %reduce-scatter.3.cloned.1.call-done = bf16[64,2048]{1,0:T(8,128)(2,1)} async-done(((bf16[256,2048]{1,0:T(8,128)(2,1)}), bf16[64,2048]{1,0:T(8,128)(2,1)}) %reduce-scatter.3.cloned.1.call-update) | async-done | bytes 262160 | tf_op jit(solution)/shard_map/reduce_scatter | solution.py:52
  39.2 1.2 multiply_reduce_fusion.1
  40.4 1.8 fusion.29
  42.3 0.0 reduce-scatter.5.cloned.1.call-start
  42.3 1.5 collective-permute-start
  43.9 0.7 fusion.37
  44.5 0.3 reduce_window_sum.26
  44.9 0.1 broadcast_bitcast_fusion
  44.9 0.1 add_bitcast_fusion
  45.0 0.8 fusion.36
  45.8 3.2 collective-permute-done
  49.0 6.4 %collective-permute-done.1 = s32[256,8]{0,1:T(8,128)S(1)} collective-permute-done((s32[256,8]{0,1:T(8,128)S(1)}, s32[256,8]{0,1:T(8,128)S(1)}, u32[]{:S(2)}, u32[]{:S(2)}) %collective-permute-start.1) | collective-permute-done | bytes 8224 | tf_op jit(solution)/shard_map/ppermute | solution.py:70
  55.4 6.4 collective-permute-done.2
  61.8 0.1 add_select_fusion
  61.9 6.2 collective-permute-done.3
  68.1 0.3 select_reduce_fusion.2
  68.5 6.1 collective-permute-done.4
  74.6 6.3 collective-permute-done.5
  81.0 0.1 copy.88
  81.1 0.6 gather_fusion
  81.7 5.7 collective-permute-done.6
  87.4 0.7 constant_dynamic-update-slice_fusion.8
  88.2 0.7 constant_dynamic-update-slice_fusion
  88.9 0.3 copy.65
  89.2 0.5 eq.119
  89.7 0.8 select_reduce_fusion.1
  90.6 0.1 copy.66
  90.7 0.1 copy.87
  90.8 2.5 fusion.14
  93.3 1.1 broadcast_add_fusion
  94.4 11.7 %select_reduce_fusion = s32[32,512]{0,1:T(8,128)S(1)} fusion(s32[32,512,128]{2,0,1:T(8,128)S(1)} %bitcast.112, s32[32,512]{0,1:T(8,128)S(1)} %copy.66), kind=kLoop, calls=%fused_computation.23 | loop fusion | flops 6275072 | bytes 8519680 | tf_op jit(solution)/shard_map/reduce_sum | solution.py:87
  106.1 0.1 copy.68
  106.2 0.7 broadcast_add_fusion.1
  106.8 0.1 copy.89
  106.9 0.6 compare_select_fusion
  107.5 60.5 %scatter_custom_fusion = s32[5120]{0:T(1024)S(1)} fusion(s32[16384]{0:T(1024)S(1)} %bitcast.120, s32[16384]{0:T(1024)S(1)} %bitcast.119, s32[]{:T(128)} %constant.140.clone.1), kind=kCustom, calls=%fused_computation.91 | custom fusion | bytes 20484 | tf_op jit(solution)/shard_map/scatter | solution.py:101
  168.0 0.3 broadcast_in_dim.96
  168.3 0.0 all-gather.2.cloned.1.call-done
  168.4 43.3 %gather_fusion.1 = bf16[5120,2048]{1,0:T(8,128)(2,1)} fusion(bf16[2048,2048]{1,0:T(8,128)(2,1)} %all-gather.2.cloned.1.call-done, s32[5120]{0:T(1024)S(1)} %fusion.38), kind=kCustom, calls=%fused_computation.1 | custom fusion | bytes 41963520 | tf_op jit(solution)/shard_map/jit(_take)/gather | solution.py:103
  211.7 34.0 %gather.14 = bf16[8,4,16,10,2048]{4,3,2,1,0:T(8,128)(2,1)} reshape(bf16[5120,2048]{1,0:T(8,128)(2,1)} %gather_fusion.1) | data formatting | bytes 41943040 | tf_op jit(solution)/shard_map/jit(_take)/gather | solution.py:103
  245.7 20.7 %fusion = f32[16,8,4,10,256]{4,3,2,1,0:T(8,128)} fusion(bf16[16,3,2048,256]{3,2,1,0:T(8,128)(2,1)} %param.16, bf16[8,4,16,10,2048]{4,3,2,1,0:T(8,128)(2,1)} %gather.14, pred[8,4,16,10]{3,2,1,0:T(8,128)(4,1)S(1)} %broadcast_in_dim.96), kind=kOutput, calls=%fused_computation.6 | convolution fusion | flops 5379194880 | bytes 55579648 | tf_op jit(solution)/shard_map/nqsmd,sdf->nqsmf/dot_general | solution.py:18
  266.4 39.2 %convert_bitcast_fusion = bf16[8,4,16,10,2048]{4,3,1,0,2:T(8,128)(2,1)} fusion(bf16[16,3,2048,256]{3,2,1,0:T(8,128)(2,1)} %param.16, f32[16,8,4,10,256]{4,3,2,1,0:T(8,128)} %fusion, bf16[8,4,16,10,2048]{4,3,2,1,0:T(8,128)(2,1)} %gather.14, pred[8,4,16,10]{3,2,1,0:T(8,128)(4,1)S(1)} %broadcast_in_dim.96), kind=kOutput, calls=%fused_computation.4 | convolution fusion | flops 10766254080 | bytes 96474112 | tf_op jit(solution)/shard_map/nqsmf,sdf->nqsmd/dot_general | solution.py:22
  305.6 24.3 %copy.74 = bf16[8,4,16,10,2048]{4,2,3,0,1:T(8,128)(2,1)} copy(bf16[8,4,16,10,2048]{4,3,1,0,2:T(8,128)(2,1)} %convert_bitcast_fusion) | data formatting | bytes 41943040 | tf_op jit(solution)/shard_map/convert_element_type | solution.py:112
  330.0 149.5 %reduce-scatter.5.cloned.1.call-done = bf16[8,1,16,10,2048]{4,2,3,0,1:T(8,128)(2,1)} async-done(((bf16[8,4,16,10,2048]{4,2,3,0,1:T(8,128)(2,1)}), bf16[8,1,16,10,2048]{4,2,3,0,1:T(8,128)(2,1)}) %reduce-scatter.5.cloned.1.call-update) | async-done | bytes 5242896 | tf_op jit(solution)/shard_map/reduce_scatter | solution.py:111
  479.5 5.5 all-to-all-start
  485.0 0.1 constant_dynamic-slice_fusion.1
  485.1 0.1 copy.62
  485.2 0.8 compare_select_fusion.6
  486.0 0.7 fusion.30
  486.7 0.2 select_reduce_fusion.3
  486.9 0.1 copy.64
  487.0 0.1 reduce_max.9
  487.1 0.1 copy.80
  487.3 113.5 %all-to-all-done = bf16[8,1,16,10,2048]{4,2,3,1,0:T(8,128)(2,1)} async-done(((bf16[8,1,16,10,2048]{4,2,3,1,0:T(8,128)(2,1)}), bf16[8,1,16,10,2048]{4,2,3,1,0:T(8,128)(2,1)}, u32[]{:S(2)}, u32[]{:S(2)}) %all-to-all-start) | async-done | bytes 5242912 | tf_op jit(solution)/shard_map/all_to_all | solution.py:114
  600.7 9.7 %copy.76 = bf16[8,1,16,10,2048]{4,3,2,0,1:T(8,128)(2,1)} copy(bf16[8,1,16,10,2048]{4,2,3,1,0:T(8,128)(2,1)} %all-to-all-done) | data formatting | bytes 10485760 | tf_op jit(solution)/shard_map/all_to_all | solution.py:114
  610.5 10.0 %reshape.449 = bf16[1280,2048]{1,0:T(8,128)(2,1)} reshape(bf16[8,1,16,10,2048]{4,3,2,0,1:T(8,128)(2,1)} %copy.76) | data formatting | bytes 10485760 | tf_op jit(solution)/shard_map/reshape | solution.py:116
  620.5 8.5 %gather_fusion.2 = bf16[512,2048]{1,0:T(8,128)(2,1)} fusion(bf16[1280,2048]{1,0:T(8,128)(2,1)} %reshape.449, s32[1024]{0:T(1024)S(1)} %pad_clamp_fusion), kind=kCustom, calls=%fused_computation.2 | custom fusion | bytes 4196352 | tf_op jit(solution)/shard_map/gather | solution.py:116
  628.9 2.3 fusion.27
  631.2 0.3 multiply_reduce_fusion
  631.6 0.9 multiply_multiply_fusion
  (68 shorter events, 0.3 us)
Async XLA Ops:
  7.2 1.6 copy-start
  7.2 32.0 %reduce-scatter.3.cloned.1.call-start = ((), (), s32[]{:S(2)}) async-start(), calls=%async_computation.3 | async-start | bytes 1310720 | tf_op jit(solution)/shard_map/reduce_scatter | solution.py:52
  11.4 156.9 %all-gather.2.cloned.1.call-start = ((), (), s32[]{:S(2)}) async-start(), calls=%async_computation.4 | async-start | bytes 8650752 | tf_op jit(solution)/shard_map/all_gather | solution.py:66
  40.4 4.1 copy-start.11
  42.3 437.2 %reduce-scatter.5.cloned.1.call-start = ((), (), s32[]{:S(2)}) async-start(), calls=%async_computation.5 | async-start | bytes 26214400 | tf_op jit(solution)/shard_map/reduce_scatter | solution.py:111
  42.3 6.6 %collective-permute-start = (s32[256,8]{0,1:T(8,128)}, s32[256,8]{0,1:T(8,128)S(1)}, u32[]{:S(2)}, u32[]{:S(2)}) collective-permute-start(s32[256,8]{0,1:T(8,128)} %param.14), channel_id=1, source_target_pairs={{0,4},{4,8},{8,12},{12,16},{16,20},{20,24},{24,28},{28,0},{1,5},{5... | collective-permute-start | bytes 24584 | tf_op jit(solution)/shard_map/ppermute | solution.py:70
  49.0 6.5 %collective-permute-start.1 = (s32[256,8]{0,1:T(8,128)S(1)}, s32[256,8]{0,1:T(8,128)S(1)}, u32[]{:S(2)}, u32[]{:S(2)}) collective-permute-start(s32[256,8]{0,1:T(8,128)S(1)} %collective-permute-done), channel_id=1, source_target_pairs={{0,4},{4,8},{8,12},{12,16},{16,20},{20,24},{24,28},{28,0},{1,5},{5... | collective-permute-start | bytes 24584 | tf_op jit(solution)/shard_map/ppermute | solution.py:70
  55.4 6.4 collective-permute-start.2
  61.8 6.3 collective-permute-start.3
  68.1 6.5 %collective-permute-start.4 = (s32[256,8]{0,1:T(8,128)S(1)}, s32[256,8]{0,1:T(8,128)S(1)}, u32[]{:S(2)}, u32[]{:S(2)}) collective-permute-start(s32[256,8]{0,1:T(8,128)S(1)} %collective-permute-done.3), channel_id=1, source_target_pairs={{0,4},{4,8},{8,12},{12,16},{16,20},{20,24},{24,28},{28,0},{1,5},{5... | collective-permute-start | bytes 24584 | tf_op jit(solution)/shard_map/ppermute | solution.py:70
  74.6 6.3 collective-permute-start.5
  81.0 6.4 %collective-permute-start.6 = (s32[256,8]{0,1:T(8,128)S(1)}, s32[256,8]{0,1:T(8,128)S(1)}, u32[]{:S(2)}, u32[]{:S(2)}) collective-permute-start(s32[256,8]{0,1:T(8,128)S(1)} %collective-permute-done.5), channel_id=1, source_target_pairs={{0,4},{4,8},{8,12},{12,16},{16,20},{20,24},{24,28},{28,0},{1,5},{5... | collective-permute-start | bytes 24584 | tf_op jit(solution)/shard_map/ppermute | solution.py:70
  90.6 3.8 copy-start.5
  329.9 155.1 %copy-start.8 = (s32[256,8]{0,1:T(8,128)S(1)}, s32[256,8]{0,1:T(8,128)}, u32[]{:S(2)}) copy-start(s32[256,8]{0,1:T(8,128)} %param.14) | copy-start | bytes 24580
  329.9 155.3 %copy-start.6 = (s32[32,512]{1,0:T(8,128)S(1)}, s32[32,512]{1,0:T(8,128)}, u32[]{:S(2)}) copy-start(s32[32,512]{1,0:T(8,128)} %copy-done.5) | copy-start | bytes 196612
  329.9 156.1 %copy-start.2 = (bf16[64,2048]{1,0:T(8,128)(2,1)S(1)}, bf16[64,2048]{1,0:T(8,128)(2,1)}, u32[]{:S(2)}) copy-start(bf16[64,2048]{1,0:T(8,128)(2,1)} %param.11) | copy-start | bytes 786436
  329.9 156.1 %copy-start.3 = (bf16[64,2048]{1,0:T(8,128)(2,1)S(1)}, bf16[64,2048]{1,0:T(8,128)(2,1)}, u32[]{:S(2)}) copy-start(bf16[64,2048]{1,0:T(8,128)(2,1)} %reduce-scatter.3.cloned.1.call-done) | copy-start | bytes 786436
  330.0 156.1 %copy-start.7 = (f32[2048,64]{0,1:T(8,128)S(1)}, f32[2048,64]{0,1:T(8,128)}, u32[]{:S(2)}) copy-start(f32[2048,64]{0,1:T(8,128)} %param.13) | copy-start | bytes 1572868
  330.0 156.1 %copy-start.9 = (f32[2048]{0:T(1024)S(1)}, f32[2048]{0:T(1024)}, u32[]{:S(2)}) copy-start(f32[2048]{0:T(1024)} %param.12) | copy-start | bytes 24580
  330.0 156.0 %copy-start.12 = (f32[64]{0:T(128)S(1)}, f32[64]{0:T(128)}, u32[]{:S(2)}) copy-start(f32[64]{0:T(128)} %copy-done.11) | copy-start | bytes 772
  479.5 121.2 %all-to-all-start = ((bf16[8,1,16,10,2048]{4,2,3,1,0:T(8,128)(2,1)}), bf16[8,1,16,10,2048]{4,2,3,1,0:T(8,128)(2,1)}, u32[]{:S(2)}, u32[]{:S(2)}) async-start(bf16[8,1,16,10,2048]{4,2,3,1,0:T(8,128)(2,1)} %bitcast.113), calls=%async_computation.2 | async-start | bytes 10485760 | tf_op jit(solution)/shard_map/all_to_all | solution.py:114
  610.5 22.0 %copy-start.1 = (bf16[512,2048]{1,0:T(8,128)(2,1)S(1)}, bf16[512,2048]{1,0:T(8,128)(2,1)}, u32[]{:S(2)}) copy-start(bf16[512,2048]{1,0:T(8,128)(2,1)} %param.10) | copy-start | bytes 6291460
  620.5 11.1 %copy-start.10 = (f32[2048]{0:T(1024)S(1)}, f32[2048]{0:T(1024)}, u32[]{:S(2)}) copy-start(f32[2048]{0:T(1024)} %param.17) | copy-start | bytes 24580
  631.5 1.0 copy-start.4
Sparse Core Ops, SparseCore 0:
  11.6 27.5 reduce-scatter.2
  43.0 77.6 all-gather.1
  330.0 149.4 reduce-scatter.4
